TPU v7x, 128 devices: a whole 4x4x4 slice. The times are simulated.
128 devices in a mesh: ctx: 16 (over x_lo, z, core), tp: 8 (over y, x_hi).
Axes of the slice: x: 4 (x_hi: 2, x_lo: 2; x = x_hi * 2 + x_lo), y: 4, z: 4, core: 2. Of those that a mesh axis runs over, the one named last changes fastest.
Arguments:
- queries: bfloat16 [8192, 4096], P('ctx', 'tp'), may hold values from -6 to 6
- key_rows: bfloat16 [8192, 4096], P('ctx', 'tp'), may hold values from -6 to 6
- value_rows: bfloat16 [8192, 4096], P('ctx', 'tp'), may hold values from -30 to 30
- selection: int32 [16, 3], replicated, may hold values from 0 to 15, as said below
- out_weight: bfloat16 [4096, 7168], P('tp'), may hold values from -0.125 to 0.125
Outputs:
- mixed: bfloat16 [8192, 7168], P('ctx', 'tp')
Inputs may be any that keep to these rules, and one draw needn't show every extreme that they name: Row q of selection lists q first, then 3 - 1 distinct blocks below q; where fewer than that lie below q, the remaining entries are q.
All inputs are finite; a program needn't handle non-finite values.
Results may differ from a plain program's by a relative error of at most 0.013.
Values may be sent and summed in bfloat16 or wider, within the bound.
No kernel may reach another device: no remote copies, remote signals or barrier semaphores. Data moves between devices by JAX's collectives and lax.ppermute only.
A program may use at most 192 MiB of HBM per device.

v0:
```python
import jax
import jax.numpy as jnp
from jax import lax
from jax.sharding import PartitionSpec as P

HD = 128
BLOCK = 512
neg_fill = -1e30


def per_device(queries, key_rows, value_rows, selection, out_weight):
    row_count, feat_width = queries.shape
    head_count = feat_width // HD
    topk = selection.shape[1]
    ctx_place = lax.axis_index("ctx")
    first_row = ctx_place * row_count
    scaling = 1.0 / jnp.sqrt(jnp.float32(HD))
    query_heads = queries.reshape(row_count, head_count, HD).transpose(1, 0, 2)
    own_choice = lax.dynamic_slice_in_dim(selection, ctx_place, 1, 0)[0]
    usable = jnp.concatenate([jnp.ones((1,), bool), own_choice[1:] != own_choice[0]])
    kv_piece = lax.all_gather(
        jnp.concatenate([key_rows, value_rows], axis=1), "ctx", axis=0, tiled=True
    )
    picked = jnp.stack(
        [lax.dynamic_slice_in_dim(kv_piece, own_choice[s] * BLOCK, BLOCK, 0) for s in range(topk)]
    ).reshape(topk * BLOCK, 2, head_count, HD)
    key_heads = picked[:, 0].transpose(1, 0, 2)
    value_heads = picked[:, 1].transpose(1, 0, 2)
    query_pos = first_row + jnp.arange(row_count, dtype=jnp.int32)
    key_pos = (own_choice[:, None] * BLOCK + jnp.arange(BLOCK, dtype=jnp.int32)[None, :]).reshape(
        -1
    )
    slot_ok = jnp.repeat(usable, BLOCK)
    allowed = (key_pos[None, :] <= query_pos[:, None]) & slot_ok[None, :]
    scores = (
        jnp.einsum("htd,hsd->hts", query_heads, key_heads, preferred_element_type=jnp.float32)
        * scaling
    )
    run_max = jnp.max(jnp.where(allowed[None], scores, neg_fill), axis=-1)
    expo = jnp.where(allowed[None], jnp.exp(scores - run_max[..., None]), 0.0)
    run_sum = jnp.sum(expo, axis=-1)
    weights = expo.astype(jnp.bfloat16)
    run_acc = jnp.einsum("hts,hsd->htd", weights, value_heads, preferred_element_type=jnp.float32)
    attended = (
        (run_acc / run_sum[..., None])
        .astype(jnp.bfloat16)
        .transpose(1, 0, 2)
        .reshape(row_count, feat_width)
    )
    shares = lax.psum_scatter(
        lax.dot_general(
            out_weight, attended, (((0,), (1,)), ((), ())), preferred_element_type=jnp.float32
        ).astype(jnp.bfloat16),
        "tp",
        scatter_dimension=0,
        tiled=True,
    ).astype(jnp.float32)
    mixed_out = jnp.transpose(shares)
    return mixed_out.astype(jnp.bfloat16)


def solution(mesh):
    placed = (P("ctx", "tp"), P("ctx", "tp"), P("ctx", "tp"), P(), P("tp", None))
    return jax.shard_map(
        per_device, mesh=mesh, in_specs=placed, out_specs=P("ctx", "tp"), check_vma=False
    )
```

profile of v0, /device:TPU:1, one launch (start us, length us, event | category | flops | bytes accessed | tf_op | source)
XLA Modules:
  0.0 271.5 jit_solution(3721377676455916608)
XLA Ops:
  6.5 0.0 copy-start
  6.5 0.0 all-gather.2.cloned.1.call-start
  6.5 2.4 pad_maximum_fusion.1
  8.9 0.0 all-gather.2.cloned.1.call-update
  8.9 0.0 reduce-scatter.4.cloned.1.call-start
  9.0 0.9 multiply_reduce_fusion
  9.8 0.6 fusion.32
  12.3 0.8 compare_reduce_fusion
  13.0 0.1 pad_add_fusion
  13.1 0.1 broadcast_in_dim.27
  13.2 0.1 iota_add_fusion
  13.3 1.1 compare_and_fusion
  14.4 89.9 %all-gather.2.cloned.1.call-done = bf16[8192,1024]{1,0:T(8,128)(2,1)} async-done(((bf16[512,1024]{1,0:T(8,128)(2,1)}), bf16[8192,1024]{1,0:T(8,128)(2,1)}) %all-gather.2.cloned.1.call-update) | async-done | bytes 16777232 | tf_op jit(solution)/shard_map/all_gather | solution.py:21
  104.4 2.2 dynamic-slice_bitcast_fusion.2
  106.6 2.0 pad_maximum_fusion
  108.7 6.1 %reshape.97 = bf16[1536,2,4,128]{3,2,1,0:T(4,128)(2,1)} reshape(bf16[3,512,1024]{2,1,0:T(8,128)(2,1)} %pad_maximum_fusion) | data formatting | bytes 6291456 | tf_op jit(solution)/shard_map/reshape | solution.py:26
  114.8 3.4 %fusion.31 = (bf16[1536,1,4,128]{3,2,1,0:T(4,128)(2,1)S(1)}, bf16[1536,1,4,128]{3,2,1,0:T(4,128)(2,1)}) fusion(bf16[1536,2,4,128]{3,2,1,0:T(4,128)(2,1)} %reshape.97), kind=kLoop, calls=%fused_computation.36 | loop fusion | bytes 6291456 | tf_op jit(solution)/shard_map/slice | solution.py:28
  118.1 2.3 copy.20
  120.4 0.0 copy-done
  120.4 3.2 %fusion.11 = f32[4,1536,512]{2,1,0:T(8,128)S(1)} fusion(bf16[1536,1,4,128]{3,2,1,0:T(4,128)(2,1)} %get-tuple-element.11, bf16[512,512]{1,0:T(8,128)(2,1)S(1)} %copy-done), kind=kOutput, calls=%fused_computation.17 | convolution fusion | flops 805306368 | bytes 14680064 | tf_op jit(solution)/shard_map/htd,hsd->hts/dot_general | solution.py:36
  123.6 8.1 %fusion.33 = (f32[4,512]{1,0:T(4,128)S(1)}, bf16[4,512,1536]{1,2,0:T(8,128)(2,1)}) fusion(f32[4,1536,512]{2,1,0:T(8,128)S(1)} %fusion.11, pred[512,1536]{0,1:T(8,128)(4,1)S(1)} %compare_and_fusion), kind=kOutput, calls=%fused_computation.38 | output fusion | flops 22021632 | bytes 19668992 | tf_op jit(solution)/shard_map/sub | solution.py:40
  131.7 4.3 %fusion.23 = bf16[512,4,128]{0,2,1:T(8,128)(2,1)S(1)} fusion(bf16[4,512,1536]{1,2,0:T(8,128)(2,1)} %get-tuple-element.16, bf16[1536,1,4,128]{0,3,2,1:T(8,128)(2,1)} %copy.20, f32[512,4]{0,1:T(4,128)S(1)} %bitcast.65), kind=kOutput, calls=%fused_computation.21 | convolution fusion | flops 805830656 | bytes 8396800 | tf_op jit(solution)/shard_map/hts,hsd->htd/dot_general | solution.py:43
  136.0 9.2 %fusion.5 = bf16[7168,512]{0,1:T(8,128)(2,1)} fusion(bf16[512,512]{0,1:T(8,128)(2,1)S(1)} %bitcast.64, bf16[512,7168]{1,0:T(8,128)(2,1)} %param.9), kind=kOutput, calls=%fused_computation.8 | convolution fusion | flops 3761766400 | bytes 15204352 | tf_op jit(solution)/shard_map/dot_general | solution.py:51
  145.2 0.0 copy-start.1
  145.2 10.5 %copy.18 = bf16[7168,512]{1,0:T(8,128)(2,1)} copy(bf16[7168,512]{0,1:T(8,128)(2,1)} %fusion.5) | data formatting | bytes 14680064
  155.7 0.0 reduce-scatter.4.cloned.1.call-update
  155.7 106.8 %reduce-scatter.4.cloned.1.call-done = bf16[896,512]{1,0:T(8,128)(2,1)} async-done(((bf16[7168,512]{1,0:T(8,128)(2,1)}), bf16[896,512]{1,0:T(8,128)(2,1)}) %reduce-scatter.4.cloned.1.call-update) | async-done | bytes 917520
  262.5 2.2 copy.19
  264.7 0.0 copy-done.1
  (3 shorter events, 0.0 us)
Async XLA Ops:
  6.5 113.9 %copy-start = (bf16[512,512]{1,0:T(8,128)(2,1)S(1)}, bf16[512,512]{1,0:T(8,128)(2,1)}, u32[]{:S(2)}) copy-start(bf16[512,512]{1,0:T(8,128)(2,1)} %param.5) | copy-start | bytes 1572868
  6.5 97.9 %all-gather.2.cloned.1.call-start = ((), (), s32[]{:S(2)}) async-start(), calls=%async_computation.1 | async-start | bytes 17825792 | tf_op jit(solution)/shard_map/all_gather | solution.py:21
  8.9 253.6 %reduce-scatter.4.cloned.1.call-start = ((), (), s32[]{:S(2)}) async-start(), calls=%async_computation.2 | async-start | bytes 8257536
  145.2 119.5 %copy-start.1 = (bf16[512,512]{1,0:T(8,128)(2,1)S(1)}, bf16[512,512]{1,0:T(8,128)(2,1)}, u32[]{:S(2)}) copy-start(bf16[512,512]{1,0:T(8,128)(2,1)} %param.5) | copy-start | bytes 1572868
Sparse Core Ops, SparseCore 0:
  9.1 95.2 all-gather.1
  155.8 106.5 reduce-scatter.3
where the time goes:
time: 272 us
  waiting for transfers between devices  197 us (72%)
  local copies, waits for them, and re-layouts  27.4 us (10%)
  matrix products  16.7 us (6%)
  other arithmetic  15.4 us (6%)
  between operations  15.3 us (6%)
    unnamed x3, waiting for transfers between devices  107 us
    all_gather x1, waiting for transfers between devices, per_device(): lax.all_gather(jnp.concatenate([key_rows, value_rows], axis=1), 'ctx', ax...  89.9 us
    unnamed x7, local copies, waits for them, and re-layouts  15 us
    dot_general x1, matrix products, per_device(): lax.dot_general(out_weight, attended, (((0,), (1,)), ((), ())), preferred...  9.24 us
    sub x1, other arithmetic, per_device(): expo = jnp.where(allowed[None], jnp.exp(scores - run_max[..., None]), 0.0)  8.07 us
    reshape x1, local copies, waits for them, and re-layouts, per_device(): picked = jnp.stack([lax.dynamic_slice_in_dim(kv_piece, own_choice[s] * BL...  6.08 us
  transfers between devices with their start and end apart: 2, of which 2 were waited for; matrix products, arithmetic and copies ran while one was open for 1% of the time, Pallas kernels for 0%

commit v1 on v0

--- a/solution.py
+++ b/solution.py
@@ -1,11 +1,23 @@
+import functools
 import jax
 import jax.numpy as jnp
 from jax import lax
 from jax.sharding import PartitionSpec as P
+from jax.lax import all_to_all, axis_size
 
 HD = 128
 BLOCK = 512
 neg_fill = -1e30
+
+
+def quotas_change(inner_x, a_name, out_dim):
+    piece_next = jnp.concatenate(
+        all_to_all(jnp.stack([inner_x] * axis_size(a_name)), a_name, 0, 0), axis=out_dim
+    )
+    return piece_next
+
+
+_apply_ends = functools.partial(quotas_change, a_name="ctx", out_dim=0)
 
 
 def per_device(queries, key_rows, value_rows, selection, out_weight):
@@ -18,9 +30,7 @@
     query_heads = queries.reshape(row_count, head_count, HD).transpose(1, 0, 2)
     own_choice = lax.dynamic_slice_in_dim(selection, ctx_place, 1, 0)[0]
     usable = jnp.concatenate([jnp.ones((1,), bool), own_choice[1:] != own_choice[0]])
-    kv_piece = lax.all_gather(
-        jnp.concatenate([key_rows, value_rows], axis=1), "ctx", axis=0, tiled=True
-    )
+    kv_piece = _apply_ends(jnp.concatenate([key_rows, value_rows], axis=1))
     picked = jnp.stack(
         [lax.dynamic_slice_in_dim(kv_piece, own_choice[s] * BLOCK, BLOCK, 0) for s in range(topk)]
     ).reshape(topk * BLOCK, 2, head_count, HD)

time: 272 us -> 452 us (1.66)
  waiting for transfers between devices: 197 us -> 364 us
  starting transfers between devices: 0.04 us -> 7.93 us
  local copies, waits for them, and re-layouts: 27.4 us -> 33.4 us
    all_to_all x0 -> x1, waiting for transfers between devices: none -> 253 us  [quotas_change(): all_to_all(jnp.stack([inner_x] * axis_size(a_name)), a_name, 0, 0)]
    all_gather x1 -> x0, waiting for transfers between devices: 89.9 us -> none  [per_device(): lax.all_gather(jnp.concatenate([key_rows, value_rows], axis=1), 'ctx', ax...]
    all_to_all x0 -> x1, starting transfers between devices: none -> 7.89 us  [quotas_change(): all_to_all(jnp.stack([inner_x] * axis_size(a_name)), a_name, 0, 0)]
    another operation x0 -> x1, local copies, waits for them, and re-layouts: none -> 5.99 us  [quotas_change(): jnp.stack([inner_x] * axis_size(a_name))]
    unnamed x3 -> x2, waiting for transfers between devices: 107 us -> 111 us
    unnamed x7 -> x9, local copies, waits for them, and re-layouts: 15 us -> 15 us
where the time goes in v1:
time: 452 us; the launch traced here: 451 us
  waiting for transfers between devices  364 us (81%)
  local copies, waits for them, and re-layouts  33.4 us (7%)
  matrix products  16.7 us (4%)
  between operations  15.5 us (3%)
  other arithmetic  13.7 us (3%)
  starting transfers between devices  7.93 us (2%)
    all_to_all x1, waiting for transfers between devices, quotas_change(): all_to_all(jnp.stack([inner_x] * axis_size(a_name)), a_name, 0, 0)  253 us
    unnamed x2, waiting for transfers between devices  111 us
    unnamed x9, local copies, waits for them, and re-layouts  15 us
    dot_general x1, matrix products, per_device(): lax.dot_general(out_weight, attended, (((0,), (1,)), ((), ())), preferred...  9.24 us
  transfers between devices with their start and end apart: 2, of which 2 were waited for; matrix products, arithmetic and copies ran while one was open for 1% of the time, Pallas kernels for 0%

profile of v1, /device:TPU:1, one launch (start us, length us, event | category | flops | bytes accessed | tf_op | source)
XLA Modules:
  0.0 451.1 jit_solution(926638672040405668)
XLA Ops:
  6.5 0.0 copy-start
  6.5 1.4 pad_maximum_fusion.1
  7.9 6.0 %stack.10 = bf16[16,512,1024]{2,1,0:T(8,128)(2,1)} broadcast(bf16[512,1024]{1,0:T(8,128)(2,1)S(1)} %pad_maximum_fusion.1), dimensions={1,2} | broadcast | bytes 17825792 | tf_op jit(solution)/shard_map/stack | solution.py:15
  13.9 0.0 copy-start.2
  13.9 7.9 %all-to-all-start = ((bf16[16,512,1024]{2,1,0:T(8,128)(2,1)}), bf16[16,512,1024]{2,1,0:T(8,128)(2,1)}, u32[]{:S(2)}, u32[]{:S(2)}) async-start(bf16[16,512,1024]{2,1,0:T(8,128)(2,1)} %stack.10), calls=%async_computation | async-start | bytes 33554432 | tf_op jit(solution)/shard_map/all_to_all | solution.py:15
  21.8 0.0 reduce-scatter.4.cloned.1.call-start
  21.8 0.0 copy-done.2
  21.8 0.2 multiply_reduce_fusion
  22.0 0.6 fusion.32
  24.7 0.1 iota_add_fusion
  24.7 0.8 compare_reduce_fusion
  25.5 0.1 pad_add_fusion
  25.6 0.1 broadcast_in_dim.27
  25.7 1.1 compare_and_fusion
  26.8 253.3 %all-to-all-done = bf16[16,512,1024]{2,1,0:T(8,128)(2,1)} async-done(((bf16[16,512,1024]{2,1,0:T(8,128)(2,1)}), bf16[16,512,1024]{2,1,0:T(8,128)(2,1)}, u32[]{:S(2)}, u32[]{:S(2)}) %all-to-all-start) | async-done | bytes 16777248 | tf_op jit(solution)/shard_map/all_to_all | solution.py:15
  280.1 2.2 dynamic-slice_bitcast_fusion.2
  282.4 2.0 pad_maximum_fusion
  284.4 6.1 %reshape.103 = bf16[1536,2,4,128]{3,2,1,0:T(4,128)(2,1)} reshape(bf16[3,512,1024]{2,1,0:T(8,128)(2,1)} %pad_maximum_fusion) | data formatting | bytes 6291456 | tf_op jit(solution)/shard_map/reshape | solution.py:36
  290.5 3.4 fusion.31
  293.9 2.3 copy.20
  296.2 0.0 copy-done
  296.2 3.2 fusion.11
  299.4 8.1 %fusion.33 = (f32[4,512]{1,0:T(4,128)S(1)}, bf16[4,512,1536]{1,2,0:T(8,128)(2,1)}) fusion(f32[4,1536,512]{2,1,0:T(8,128)S(1)} %fusion.11, pred[512,1536]{0,1:T(8,128)(4,1)S(1)} %compare_and_fusion), kind=kOutput, calls=%fused_computation.38 | output fusion | flops 22021632 | bytes 19668992 | tf_op jit(solution)/shard_map/sub | solution.py:50
  307.5 4.3 fusion.23
  311.7 9.2 %fusion.5 = bf16[7168,512]{0,1:T(8,128)(2,1)} fusion(bf16[512,512]{0,1:T(8,128)(2,1)S(1)} %bitcast.65, bf16[512,7168]{1,0:T(8,128)(2,1)} %param.9), kind=kOutput, calls=%fused_computation.8 | convolution fusion | flops 3761766400 | bytes 15204352 | tf_op jit(solution)/shard_map/dot_general | solution.py:61
  321.0 0.0 copy-start.1
  321.0 10.5 %copy.18 = bf16[7168,512]{1,0:T(8,128)(2,1)} copy(bf16[7168,512]{0,1:T(8,128)(2,1)} %fusion.5) | data formatting | bytes 14680064
  331.4 0.0 reduce-scatter.4.cloned.1.call-update
  331.5 110.6 %reduce-scatter.4.cloned.1.call-done = bf16[896,512]{1,0:T(8,128)(2,1)} async-done(((bf16[7168,512]{1,0:T(8,128)(2,1)}), bf16[896,512]{1,0:T(8,128)(2,1)}) %reduce-scatter.4.cloned.1.call-update) | async-done | bytes 917520
  442.1 2.2 copy.19
  444.3 0.0 copy-done.1
  (3 shorter events, 0.0 us)
Async XLA Ops:
  6.5 289.6 %copy-start = (bf16[512,512]{1,0:T(8,128)(2,1)S(1)}, bf16[512,512]{1,0:T(8,128)(2,1)}, u32[]{:S(2)}) copy-start(bf16[512,512]{1,0:T(8,128)(2,1)} %param.5) | copy-start | bytes 1572868
  13.9 7.9 %copy-start.2 = (s32[16,3]{0,1:T(4,128)S(1)}, s32[16,3]{0,1:T(4,128)}, u32[]{:S(2)}) copy-start(s32[16,3]{0,1:T(4,128)} %param.8) | copy-start | bytes 580
  13.9 266.2 %all-to-all-start = ((bf16[16,512,1024]{2,1,0:T(8,128)(2,1)}), bf16[16,512,1024]{2,1,0:T(8,128)(2,1)}, u32[]{:S(2)}, u32[]{:S(2)}) async-start(bf16[16,512,1024]{2,1,0:T(8,128)(2,1)} %stack.10), calls=%async_computation | async-start | bytes 33554432 | tf_op jit(solution)/shard_map/all_to_all | solution.py:15
  21.8 420.3 %reduce-scatter.4.cloned.1.call-start = ((), (), s32[]{:S(2)}) async-start(), calls=%async_computation.2 | async-start | bytes 8257536
  321.0 123.3 %copy-start.1 = (bf16[512,512]{1,0:T(8,128)(2,1)S(1)}, bf16[512,512]{1,0:T(8,128)(2,1)}, u32[]{:S(2)}) copy-start(bf16[512,512]{1,0:T(8,128)(2,1)} %param.5) | copy-start | bytes 1572868
Sparse Core Ops, SparseCore 0:
  331.6 110.4 reduce-scatter.3
